TPU v7x, 32 devices: a whole 2x2x4 slice. The times are simulated.
32 devices in a mesh: gx: 4 (over y, x), gy: 2 (over core), gz: 4 (over z).
Axes of the slice: x: 2, y: 2, z: 4, core: 2. Of those that a mesh axis runs over, the one named last changes fastest.
Arguments:
- features: bfloat16 [8, 32, 65536], P('gz', 'gy', 'gx'), may hold values from -6 to 6
- depth_weight: bfloat16 [27, 64], replicated, may hold values from -1.25 to 1.25
- expand_weight: bfloat16 [64, 256], replicated, may hold values from -0.75 to 0.75
- project_weight: bfloat16 [256, 64], replicated, may hold values from -0.375 to 0.375
- spec_real: bfloat16 [32, 64, 64], replicated, may hold values from -2 to 2
- spec_imag: bfloat16 [32, 64, 64], replicated, may hold values from -2 to 2
- cotangent: bfloat16 [8, 32, 65536], P('gz', 'gy', 'gx'), may hold values from -6 to 6
Outputs:
- output: bfloat16 [8, 32, 65536], P('gz', 'gy', 'gx')
- grad_features: bfloat16 [8, 32, 65536], P('gz', 'gy', 'gx')
- grad_spec: float32 [2, 32, 64, 64], P(None, 'gx')
All inputs are finite; a program needn't handle non-finite values.
Results may differ from a plain program's by a relative error of at most 0.018.
Values may be sent and summed in bfloat16 or wider, within the bound.
No kernel may reach another device: no remote copies, remote signals or barrier semaphores. Data moves between devices by JAX's collectives and lax.ppermute only.
A program may use at most 64 MiB of HBM per device.

v0:
```python
import math
import jax
import jax.numpy as jnp
from jax import lax
from jax.sharding import PartitionSpec as P


def padded_2(value, sides, width, wrap):
    for axis, dim in sides:
        size, length = (lax.axis_size(axis), value.shape[dim])
        up = [(i, (i + 1) % size) for i in range(size if wrap else size - 1)]
        down = [(j, i) for i, j in up]
        last = lax.slice_in_dim(value, length - width, length, axis=dim)
        leading = lax.slice_in_dim(value, 0, width, axis=dim)
        before = lax.ppermute(last, axis, up)
        after = lax.ppermute(leading, axis, down)
        value = jnp.concatenate([before, value, after], axis=dim)
    return value


def gelu_parts(values):
    normal_cdf = 0.5 * (1.0 + jax.scipy.special.erf(values * (1.0 / math.sqrt(2.0))))
    density = jnp.exp(-0.5 * values * values) * (1.0 / math.sqrt(2.0 * math.pi))
    return (values * normal_cdf, normal_cdf + values * density)


def dft_tables(offset, cells, x_length, mode_count):
    position = offset + jnp.arange(cells, dtype=jnp.int32)
    frequency = jnp.arange(mode_count, dtype=jnp.int32)
    phase_int = position[:, None] * frequency[None, :] % x_length
    angles = phase_int.astype(jnp.float32) * (2.0 * math.pi / x_length)
    return (jnp.cos(angles).astype(jnp.bfloat16), (-jnp.sin(angles)).astype(jnp.bfloat16))


def scaled_table(table, mode_count, x_length):
    frequency = jnp.arange(mode_count, dtype=jnp.int32)
    mode_scale = jnp.where(frequency == 0, 1.0, 2.0).astype(jnp.float32) / x_length
    return (table.astype(jnp.float32) * mode_scale[None, :]).astype(jnp.bfloat16)


def block_weights(spec_real, spec_imag):
    upper_row = jnp.concatenate([spec_real, spec_imag], axis=2)
    lower_row = jnp.concatenate([-spec_imag, spec_real], axis=2)
    return jnp.concatenate([upper_row, lower_row], axis=1)


def spatial_rims(field_block, channels):
    x_wide = padded_2(field_block, (("gx", 2),), channels, True)
    return padded_2(x_wide, (("gy", 1), ("gz", 0)), 1, False)


def depthwise(padded, taps, flipped, x_cells, channels):
    planes = padded.shape[0] - 2
    y_cells = padded.shape[1] - 2
    running = jnp.zeros((planes, y_cells, x_cells * channels), jnp.float32)
    direction = -1 if flipped else 1
    for step_z in (-1, 0, 1):
        for step_y in (-1, 0, 1):
            for step_x in (-1, 0, 1):
                tap_gain = taps[(step_z + 1) * 9 + (step_y + 1) * 3 + (step_x + 1)].astype(
                    jnp.float32
                )
                z_offset = 1 + direction * step_z
                y_offset = 1 + direction * step_y
                x_offset = 1 + direction * step_x
                cut = padded[
                    z_offset : z_offset + planes,
                    y_offset : y_offset + y_cells,
                    x_offset * channels : (x_offset + x_cells) * channels,
                ]
                running = running + cut.astype(jnp.float32) * jnp.tile(tap_gain, x_cells)
    return running


def share_terms(field3, cos_table, sin_table):
    real_part = jnp.einsum("rxc,xk->krc", field3, cos_table, preferred_element_type=jnp.float32)
    imag_part = jnp.einsum("rxc,xk->krc", field3, sin_table, preferred_element_type=jnp.float32)
    return lax.psum_scatter(
        jnp.concatenate([real_part, imag_part], axis=2), "gx", scatter_dimension=0, tiled=True
    )


def share_inverse(modes_share, cos_table, sin_table, channels):
    segment = lax.all_gather(modes_share, "gx", axis=0, tiled=True)
    running = jnp.einsum(
        "krc,xk->rxc", segment[:, :, :channels], cos_table, preferred_element_type=jnp.float32
    )
    return running + jnp.einsum(
        "krc,xk->rxc", segment[:, :, channels:], sin_table, preferred_element_type=jnp.float32
    )


def split_gradients(dblock, channels):
    grad_real = dblock[:, :channels, :channels] + dblock[:, channels:, channels:]
    grad_imag = dblock[:, :channels, channels:] - dblock[:, channels:, :channels]
    return jnp.stack([grad_real, grad_imag])


def sum_gradients(local_grads):
    return lax.psum(local_grads.astype(jnp.bfloat16), ("gy", "gz")).astype(jnp.float32)


def per_device(
    features, depth_weight, expand_weight, project_weight, spec_real, spec_imag, cotangent
):
    planes, y_cells, merged = features.shape
    channels = depth_weight.shape[1]
    x_cells = merged // channels
    row_count = planes * y_cells
    mode_count = spec_real.shape[0]
    group_size = lax.axis_size("gx")
    x_length = x_cells * group_size
    x_start = lax.axis_index("gx") * x_cells
    cos_part, sin_part = dft_tables(x_start, x_cells, x_length, mode_count)
    cos_scaled = scaled_table(cos_part, mode_count, x_length)
    sin_scaled = scaled_table(sin_part, mode_count, x_length)
    blocks = block_weights(spec_real, spec_imag)
    padded = spatial_rims(features, channels)
    activation = depthwise(padded, depth_weight, False, x_cells, channels).astype(jnp.bfloat16)
    activation = activation.reshape(row_count * x_cells, channels)
    hidden_pre = jnp.dot(activation, expand_weight, preferred_element_type=jnp.float32)
    hidden, hidden_slope = gelu_parts(hidden_pre)
    local_branch = jnp.dot(
        hidden.astype(jnp.bfloat16), project_weight, preferred_element_type=jnp.float32
    )
    local_branch = local_branch.reshape(row_count, x_cells, channels)
    field3 = features.reshape(row_count, x_cells, channels)
    share_size = mode_count // group_size
    owned_blocks = lax.dynamic_slice_in_dim(
        blocks, lax.axis_index("gx") * share_size, share_size, 0
    )
    coeffs = share_terms(field3, cos_part, sin_part).astype(jnp.bfloat16)
    mixed_modes = jnp.einsum(
        "krc,kco->kro", coeffs, owned_blocks, preferred_element_type=jnp.float32
    ).astype(jnp.bfloat16)
    spectral = share_inverse(mixed_modes, cos_scaled, sin_scaled, channels)
    result, slopes = gelu_parts(local_branch + spectral)
    output = result.astype(jnp.bfloat16).reshape(planes, y_cells, merged)
    grad_pre = (
        cotangent.reshape(row_count, x_cells, channels).astype(jnp.float32) * slopes
    ).astype(jnp.bfloat16)
    hidden_grad = jnp.dot(
        grad_pre.reshape(row_count * x_cells, channels),
        project_weight.T,
        preferred_element_type=jnp.float32,
    )
    grad_hidden = (hidden_grad * hidden_slope).astype(jnp.bfloat16)
    grad_act = jnp.dot(grad_hidden, expand_weight.T, preferred_element_type=jnp.float32).astype(
        jnp.bfloat16
    )
    grad_act = grad_act.reshape(planes, y_cells, merged)
    dcoef = share_terms(grad_pre, cos_scaled, sin_scaled).astype(jnp.bfloat16)
    dmode = jnp.einsum(
        "kro,kco->krc", dcoef, owned_blocks, preferred_element_type=jnp.float32
    ).astype(jnp.bfloat16)
    spectral_grad = share_inverse(dmode, cos_part, sin_part, channels)
    dblock = jnp.einsum("krc,kro->kco", coeffs, dcoef, preferred_element_type=jnp.float32)
    grad_spec = sum_gradients(split_gradients(dblock, channels))
    padded_grad = spatial_rims(grad_act, channels)
    grad_local = depthwise(padded_grad, depth_weight, True, x_cells, channels)
    grad_features = (grad_local + spectral_grad.reshape(planes, y_cells, merged)).astype(
        jnp.bfloat16
    )
    return (output, grad_features, grad_spec)


def solution(mesh):
    placed = (P("gz", "gy", "gx"), P(), P(), P(), P(), P(), P("gz", "gy", "gx"))
    return jax.shard_map(
        per_device,
        mesh=mesh,
        in_specs=placed,
        out_specs=(P("gz", "gy", "gx"), P("gz", "gy", "gx"), P(None, "gx", None, None)),
        check_vma=False,
    )
```

profile of v0, /device:TPU:0, one launch (start us, length us, event | category | flops | bytes accessed | tf_op | source)
XLA Modules:
  0.0 243.0 jit_solution(9802269547435364776)
XLA Ops:
  8.0 3.9 %collective-permute-start.1 = (bf16[2,16,64]{2,1,0:T(8,128)(2,1)S(1)}, bf16[2,16,64]{2,1,0:T(8,128)(2,1)S(1)}, u32[]{:S(2)}, u32[]{:S(2)}) collective-permute-start(bf16[2,16,64]{2,1,0:T(8,128)(2,1)S(1)} %get-tuple-element.19), channel_id=1, source_target_pairs={{8,0},{16,8},{24,16},{0,24},{9,1},{17,9},{25,17},{1,25},{10,2},{18... | collective-permute-start | bytes 12296 | tf_op jit(solution)/shard_map/ppermute | solution.py:16
  11.9 3.0 %reshape.69 = bf16[32,256,64]{2,1,0:T(8,128)(2,1)S(1)} reshape(bf16[2,16,16384]{2,1,0:T(8,128)(2,1)} %param.7) | data formatting | bytes 2097152 | tf_op jit(solution)/shard_map/reshape | solution.py:127
  15.0 1.4 fusion.47
  16.3 1.3 fusion.50
  17.7 2.8 %concatenate.105 = bf16[2,16,16512]{2,1,0:T(8,128)(2,1)S(1)} concatenate(bf16[2,16,64]{2,1,0:T(8,128)(2,1)S(1)} %collective-permute-done, bf16[2,16,16384]{2,1,0:T(8,128)(2,1)} %param.7, bf16[2,16,64]{2,1,0:T(8,128)(2,1)S(1)} %collective-permute-done.1), dimensions={2} | concatenate | bytes 2113536 | tf_op jit(solution)/shard_map/concatenate | solution.py:17
  20.7 1.5 collective-permute-start.2
  22.2 1.3 collective-permute-start.3
  26.1 1.2 fusion.94
  27.3 4.4 %collective-permute-start.4 = (bf16[1,18,16512]{2,1,0:T(8,128)(2,1)}, bf16[1,18,16512]{2,1,0:T(8,128)(2,1)}, u32[]{:S(2)}, u32[]{:S(2)}) collective-permute-start(bf16[1,18,16512]{2,1,0:T(8,128)(2,1)} %get-tuple-element.7), channel_id=1, source_target_pairs={{0,1},{1,2},{2,3},{4,5},{5,6},{6,7},{8,9},{9,10},{10,11},{12,13},{... | collective-permute-start | bytes 1783304 | tf_op jit(solution)/shard_map/ppermute | solution.py:15
  31.7 1.5 collective-permute-start.5
  52.3 3.3 %reshape.101 = f32[32,256,64]{2,1,0:T(8,128)} reshape(bf16[2,16,16384]{2,1,0:T(8,128)(2,1)S(1)} %copy-done.13) | data formatting | bytes 3145728 | tf_op jit(solution)/shard_map/convert_element_type | solution.py:140
  55.6 3.9 %copy.44 = f32[32,256,64]{1,2,0:T(8,128)} copy(f32[32,256,64]{2,1,0:T(8,128)} %reshape.101) | data formatting | bytes 4194304 | tf_op jit(solution)/shard_map/convert_element_type | solution.py:140
  59.9 3.0 %maximum_maximum_fusion = (bf16[3,18,16512]{2,1,0:T(8,128)(2,1)S(1)}, bf16[3,18,16512]{2,1,0:T(8,128)(2,1)S(1)}) fusion(bf16[2,1,16512]{2,1,0:T(2,128)(2,1)S(1)} %collective-permute-done.3, bf16[2,16,16512]{2,1,0:T(8,128)(2,1)S(1)} %concatenate.105, bf16[2,1,16512]{2,1,0:T(2,128)(2,1)S(1)} %collective-permute-done.2, ...), kind=kLoop, calls=%fused_computation.12 | loop fusion | flops 14266368 | bytes 5944320 | tf_op jit(solution)/shard_map/concatenate | solution.py:17
  63.2 14.8 %add_convert_fusion.1 = bf16[2,16,16384]{2,1,0:T(8,128)(2,1)} fusion(bf16[2,16,16384]{2,1,0:T(8,128)(2,1)S(1)} %copy-done.3, bf16[2,16,16512]{2,1,0:T(8,128)(2,1)S(1)} %concatenate.105, bf16[2,1,16512]{2,1,0:T(2,128)(2,1)S(1)} %collective-permute-done.3, bf16[2,1,16512]{2,1,0:T(2,128)(2,1)S(1)} %collective-permute-done.2, ...), kind=kLoop, calls=%fused_computation.35 | loop fusion | flops 55050240 | bytes 23938048 | tf_op jit(solution)/shard_map/convert_element_type | solution.py:119
  78.0 3.0 %reshape.67 = bf16[8192,64]{1,0:T(8,128)(2,1)S(1)} reshape(bf16[2,16,16384]{2,1,0:T(8,128)(2,1)} %add_convert_fusion.1) | data formatting | bytes 2097152 | tf_op jit(solution)/shard_map/reshape | solution.py:120
  81.0 1.2 fusion.101
  82.3 3.3 %copy-done.2 = f32[8192,256]{1,0:T(8,128)} copy-done((f32[8192,256]{1,0:T(8,128)}, f32[8192,256]{1,0:T(8,128)S(1)}, u32[]{:S(2)}) %copy-start.2) | copy-done | bytes 8388632
  85.6 3.4 %fusion.5 = f32[8192,64]{0,1:T(8,128)} fusion(bf16[256,64]{0,1:T(8,128)(2,1)S(1)} %copy-done.44, f32[8192,256]{1,0:T(8,128)S(1)} %fusion.101), kind=kOutput, calls=%fused_computation.10 | convolution fusion | flops 278921216 | bytes 10518528 | tf_op jit(solution)/shard_map/dot_general | solution.py:123
  90.9 9.6 %all_gather.6 = bf16[32,32,128]{2,1,0:T(8,128)(2,1)S(1)} all-gather(bf16[8,32,128]{2,1,0:T(8,128)(2,1)S(1)} %convolution_convert_fusion.2), channel_id=1, replica_groups=mesh['gx'=4,'gy'=2,'gz'=4] {'gx'}, dimensions={0}, use_global_device_ids=true | all-gather | bytes 327680 | tf_op jit(solution)/shard_map/all_gather | solution.py:84
  101.2 2.5 %fusion.11 = (bf16[32,256,64]{1,2,0:T(8,128)(2,1)S(1)}, bf16[32,256,64]{1,2,0:T(8,128)(2,1)}) fusion(f32[32,256,64]{1,2,0:T(8,128)S(1)} %copy-done.5, f32[256,32,64]{0,2,1:T(8,128)S(1)} %fusion.29, bf16[32,32,64]{2,1,0:T(8,128)(2,1)S(1)} %get-tuple-element.25, f32[32]{0:T(128)S(1)} %fusion.66, s32[256]{0:T(256)S(1)} %iota_add_fusion, ...), kind=kOutput, calls=%fused_computation.29 | convolution fusion | flops 41050112 | bytes 8520832 | tf_op jit(solution)/shard_map/krc,xk->rxc/dot_general | solution.py:88
  104.5 7.8 %convolution_convert_fusion = bf16[8192,64]{0,1:T(8,128)(2,1)S(1)} fusion(bf16[64,256]{1,0:T(8,128)(2,1)S(1)} %copy-done, bf16[8192,64]{0,1:T(8,128)(2,1)S(1)} %bitcast.128, bf16[256,64]{0,1:T(8,128)(2,1)S(1)} %copy-done.45, f32[8192,256]{1,0:T(8,128)} %copy-done.2), kind=kOutput, calls=%fused_computation.3 | convolution fusion | flops 558366720 | bytes 10551296 | tf_op jit(solution)/shard_map/dot_general | solution.py:148
  112.4 1.8 copy.46
  114.2 2.8 %reshape.72 = bf16[2,16,16384]{2,1,0:T(8,128)(2,1)S(1)} reshape(bf16[8192,64]{1,0:T(8,128)(2,1)} %copy.46) | data formatting | bytes 2097152 | tf_op jit(solution)/shard_map/reshape | solution.py:151
  117.1 1.5 collective-permute-start.7
  119.1 1.6 collective-permute-done.7
  120.8 2.4 collective-permute-done.6
  123.1 1.1 concatenate.117
  124.5 1.3 collective-permute-start.9
  125.8 3.0 %collective-permute-start.8 = (bf16[2,1,16512]{2,1,0:T(2,128)(2,1)S(1)}, bf16[2,1,16512]{2,1,0:T(2,128)(2,1)S(1)}, u32[]{:S(2)}, u32[]{:S(2)}) collective-permute-start(bf16[2,1,16512]{2,1,0:T(2,128)(2,1)S(1)} %get-tuple-element.14), channel_id=1, source_target_pairs={{0,4},{1,5},{2,6},{3,7},{8,12},{9,13},{10,14},{11,15},{16,20},{17,... | collective-permute-start | bytes 198152 | tf_op jit(solution)/shard_map/ppermute | solution.py:15
  130.4 1.3 fusion.93
  131.7 1.3 collective-permute-start.10
  133.0 6.1 %collective-permute-start.11 = (bf16[1,18,16512]{2,1,0:T(8,128)(2,1)}, bf16[1,18,16512]{2,1,0:T(8,128)(2,1)}, u32[]{:S(2)}, u32[]{:S(2)}) collective-permute-start(bf16[1,18,16512]{2,1,0:T(8,128)(2,1)} %get-tuple-element.6), channel_id=1, source_target_pairs={{0,1},{1,2},{2,3},{4,5},{5,6},{6,7},{8,9},{9,10},{10,11},{12,13},{... | collective-permute-start | bytes 1783304 | tf_op jit(solution)/shard_map/ppermute | solution.py:15
  141.5 2.0 copy.43
  143.6 2.5 %reshape.70 = bf16[2,16,16384]{2,1,0:T(8,128)(2,1)} reshape(bf16[32,256,64]{2,1,0:T(8,128)(2,1)S(1)} %copy.43) | data formatting | bytes 2097152 | tf_op jit(solution)/shard_map/reshape | solution.py:138
  146.1 8.7 %collective-permute-done.10 = bf16[1,18,16512]{2,1,0:T(8,128)(2,1)} collective-permute-done((bf16[1,18,16512]{2,1,0:T(8,128)(2,1)}, bf16[1,18,16512]{2,1,0:T(8,128)(2,1)}, u32[]{:S(2)}, u32[]{:S(2)}) %collective-permute-start.10) | collective-permute-done | bytes 594464 | tf_op jit(solution)/shard_map/ppermute | solution.py:16
  154.8 1.2 collective-permute-done.11
  156.0 3.9 %pad_maximum_fusion.1 = (bf16[3,18,16512]{2,1,0:T(8,128)(2,1)S(1)}, bf16[3,18,16512]{2,1,0:T(8,128)(2,1)}) fusion(bf16[1,18,16512]{2,1,0:T(8,128)(2,1)} %collective-permute-done.10, bf16[2,1,16512]{2,1,0:T(2,128)(2,1)} %copy-done.11, bf16[2,16,16512]{2,1,0:T(8,128)(2,1)S(1)} %concatenate.117, bf16[2,1,16512]{2,1,0:T(2,128)(2,1)} %copy-done.12, ...), kind=kLoop, calls=%fused_computation.14 | loop fusion | flops 14266368 | bytes 5944320 | tf_op jit(solution)/shard_map/concatenate | solution.py:17
  159.9 5.4 %reduce-scatter.5.cloned.1.call-done = f32[8,32,128]{2,0,1:T(8,128)} async-done(((f32[32,32,128]{2,0,1:T(8,128)}), f32[8,32,128]{2,0,1:T(8,128)}) %reduce-scatter.5.cloned.1.call-update) | async-done | bytes 131088 | tf_op jit(solution)/shard_map/reduce_scatter | solution.py:78
  166.2 1.2 convolution_convert_fusion.1
  167.4 1.1 fusion.33
  168.5 9.2 %all_gather.7 = bf16[32,32,128]{2,1,0:T(8,128)(2,1)S(1)} all-gather(bf16[8,32,128]{2,1,0:T(8,128)(2,1)S(1)} %convolution_convert_fusion.1), channel_id=1, replica_groups=mesh['gx'=4,'gy'=2,'gz'=4] {'gx'}, dimensions={0}, use_global_device_ids=true | all-gather | bytes 327680 | tf_op jit(solution)/shard_map/all_gather | solution.py:84
  179.6 1.6 fusion.26
  181.2 2.0 add_bitcast_fusion
  183.2 3.8 %copy.50 = f32[32,256,64]{2,1,0:T(8,128)} copy(f32[32,256,64]{1,2,0:T(8,128)} %add_bitcast_fusion) | data formatting | bytes 4194304 | tf_op jit(solution)/shard_map/add | solution.py:88
  187.0 4.0 %reshape.73 = f32[2,16,16384]{2,1,0:T(8,128)} reshape(f32[32,256,64]{2,1,0:T(8,128)} %copy.50) | data formatting | bytes 4194304 | tf_op jit(solution)/shard_map/reshape | solution.py:161
  191.0 21.6 %add_convert_fusion = bf16[2,16,16384]{2,1,0:T(8,128)(2,1)} fusion(f32[2,16,16384]{2,1,0:T(8,128)} %reshape.73, bf16[2,16,16384]{2,1,0:T(8,128)(2,1)} %copy-done.4, bf16[2,16,16512]{2,1,0:T(8,128)(2,1)S(1)} %concatenate.117, bf16[2,1,16512]{2,1,0:T(2,128)(2,1)} %copy-done.12, bf16[2,1,16512]{2,1,0:T(2,128)(2,1)} %copy-done.11, ...), kind=kLoop, calls=%fused_computation.31 | loop fusion | flops 55574528 | bytes 26035200 | tf_op jit(solution)/shard_map/convert_element_type | solution.py:161
  212.5 22.1 %all-reduce.2.cloned.1.call-done = bf16[2,8,64,64]{3,2,1,0:T(8,128)(2,1)} async-done(((bf16[2,8,64,64]{3,2,1,0:T(8,128)(2,1)}), bf16[2,8,64,64]{3,2,1,0:T(8,128)(2,1)}) %all-reduce.2.cloned.1.call-update) | async-done | bytes 131088 | tf_op jit(solution)/shard_map/psum | solution.py:100
  234.7 1.8 convert_element_type.381
  (187 shorter events, 33.7 us)
Async XLA Ops:
  7.2 73.9 %copy-start = (bf16[64,256]{1,0:T(8,128)(2,1)S(1)}, bf16[64,256]{1,0:T(8,128)(2,1)}, u32[]{:S(2)}) copy-start(bf16[64,256]{1,0:T(8,128)(2,1)} %param.9) | copy-start | bytes 98308
  7.2 81.8 %reduce-scatter.3.cloned.1.call-start = ((), (), s32[]{:S(2)}) async-start(), calls=%async_computation.2 | async-start | bytes 655360 | tf_op jit(solution)/shard_map/reduce_scatter | solution.py:78
  8.0 9.7 %collective-permute-start.1 = (bf16[2,16,64]{2,1,0:T(8,128)(2,1)S(1)}, bf16[2,16,64]{2,1,0:T(8,128)(2,1)S(1)}, u32[]{:S(2)}, u32[]{:S(2)}) collective-permute-start(bf16[2,16,64]{2,1,0:T(8,128)(2,1)S(1)} %get-tuple-element.19), channel_id=1, source_target_pairs={{8,0},{16,8},{24,16},{0,24},{9,1},{17,9},{25,17},{1,25},{10,2},{18... | collective-permute-start | bytes 12296 | tf_op jit(solution)/shard_map/ppermute | solution.py:16
  11.9 5.8 %collective-permute-start = (bf16[2,16,64]{2,1,0:T(8,128)(2,1)S(1)}, bf16[2,16,64]{2,1,0:T(8,128)(2,1)S(1)}, u32[]{:S(2)}, u32[]{:S(2)}) collective-permute-start(bf16[2,16,64]{2,1,0:T(8,128)(2,1)S(1)} %get-tuple-element.20), channel_id=1, source_target_pairs={{0,8},{8,16},{16,24},{24,0},{1,9},{9,17},{17,25},{25,1},{2,10},{10... | collective-permute-start | bytes 12296 | tf_op jit(solution)/shard_map/ppermute | solution.py:15
  17.7 5.8 %copy-start.8 = (f32[32,32,64]{2,0,1:T(8,128)S(1)}, f32[32,32,64]{2,0,1:T(8,128)}, u32[]{:S(2)}) copy-start(f32[32,32,64]{2,0,1:T(8,128)} %fusion.47) | copy-start | bytes 786436
  17.7 5.8 %copy-start.9 = (f32[32,32,64]{2,0,1:T(8,128)S(1)}, f32[32,32,64]{2,0,1:T(8,128)}, u32[]{:S(2)}) copy-start(f32[32,32,64]{2,0,1:T(8,128)} %fusion.50) | copy-start | bytes 786436
  20.7 3.9 %collective-permute-start.2 = (bf16[2,1,16512]{2,1,0:T(2,128)(2,1)S(1)}, bf16[2,1,16512]{2,1,0:T(2,128)(2,1)S(1)}, u32[]{:S(2)}, u32[]{:S(2)}) collective-permute-start(bf16[2,1,16512]{2,1,0:T(2,128)(2,1)S(1)} %get-tuple-element.15), channel_id=1, source_target_pairs={{0,4},{1,5},{2,6},{3,7},{8,12},{9,13},{10,14},{11,15},{16,20},{17,... | collective-permute-start | bytes 198152 | tf_op jit(solution)/shard_map/ppermute | solution.py:15
  22.2 3.2 %collective-permute-start.3 = (bf16[2,1,16512]{2,1,0:T(2,128)(2,1)S(1)}, bf16[2,1,16512]{2,1,0:T(2,128)(2,1)S(1)}, u32[]{:S(2)}, u32[]{:S(2)}) collective-permute-start(bf16[2,1,16512]{2,1,0:T(2,128)(2,1)S(1)} %get-tuple-element.16), channel_id=1, source_target_pairs={{4,0},{5,1},{6,2},{7,3},{12,8},{13,9},{14,10},{15,11},{20,16},{21,... | collective-permute-start | bytes 198152 | tf_op jit(solution)/shard_map/ppermute | solution.py:16
  24.5 140.8 %reduce-scatter.5.cloned.1.call-start = ((), (), s32[]{:S(2)}) async-start(), calls=%async_computation.3 | async-start | bytes 655360 | tf_op jit(solution)/shard_map/reduce_scatter | solution.py:78
  26.0 7.1 %copy-start.43 = (bf16[27,64]{1,0:T(8,128)(2,1)S(1)}, bf16[27,64]{1,0:T(8,128)(2,1)}, u32[]{:S(2)}) copy-start(bf16[27,64]{1,0:T(8,128)(2,1)} %param.8) | copy-start | bytes 10372
  27.3 32.6 %collective-permute-start.4 = (bf16[1,18,16512]{2,1,0:T(8,128)(2,1)}, bf16[1,18,16512]{2,1,0:T(8,128)(2,1)}, u32[]{:S(2)}, u32[]{:S(2)}) collective-permute-start(bf16[1,18,16512]{2,1,0:T(8,128)(2,1)} %get-tuple-element.7), channel_id=1, source_target_pairs={{0,1},{1,2},{2,3},{4,5},{5,6},{6,7},{8,9},{9,10},{10,11},{12,13},{... | collective-permute-start | bytes 1783304 | tf_op jit(solution)/shard_map/ppermute | solution.py:15
  31.7 28.2 %collective-permute-start.5 = (bf16[1,18,16512]{2,1,0:T(8,128)(2,1)}, bf16[1,18,16512]{2,1,0:T(8,128)(2,1)}, u32[]{:S(2)}, u32[]{:S(2)}) collective-permute-start(bf16[1,18,16512]{2,1,0:T(8,128)(2,1)} %get-tuple-element.8), channel_id=1, source_target_pairs={{1,0},{2,1},{3,2},{5,4},{6,5},{7,6},{9,8},{10,9},{11,10},{13,12},{... | collective-permute-start | bytes 1783304 | tf_op jit(solution)/shard_map/ppermute | solution.py:16
  42.7 9.5 %copy-start.10 = (bf16[32,64,64]{2,1,0:T(8,128)(2,1)S(1)}, bf16[32,64,64]{2,1,0:T(8,128)(2,1)}, u32[]{:S(2)}) copy-start(bf16[32,64,64]{2,1,0:T(8,128)(2,1)} %param.12) | copy-start | bytes 786436
  44.9 7.4 %copy-start.13 = (bf16[2,16,16384]{2,1,0:T(8,128)(2,1)S(1)}, bf16[2,16,16384]{2,1,0:T(8,128)(2,1)}, u32[]{:S(2)}) copy-start(bf16[2,16,16384]{2,1,0:T(8,128)(2,1)} %param.13) | copy-start | bytes 3145732
  55.6 3.9 %copy-start.42 = (bf16[32,64,64]{2,1,0:T(8,128)(2,1)S(1)}, bf16[32,64,64]{2,1,0:T(8,128)(2,1)}, u32[]{:S(2)}) copy-start(bf16[32,64,64]{2,1,0:T(8,128)(2,1)} %param.11) | copy-start | bytes 786436
  59.6 30.5 %copy-start.6 = (bf16[8,128,128]{2,1,0:T(8,128)(2,1)}, bf16[8,128,128]{2,1,0:T(8,128)(2,1)S(1)}, u32[]{:S(2)}) copy-start(bf16[8,128,128]{2,1,0:T(8,128)(2,1)S(1)} %fusion.21) | copy-start | bytes 786436
  59.6 3.3 %copy-start.3 = (bf16[2,16,16384]{2,1,0:T(8,128)(2,1)S(1)}, bf16[2,16,16384]{2,1,0:T(8,128)(2,1)}, u32[]{:S(2)}) copy-start(bf16[2,16,16384]{2,1,0:T(8,128)(2,1)} %param.7) | copy-start | bytes 3145732
  59.6 3.3 %copy-start.15 = (f32[16384]{0:T(1024)S(1)}, f32[16384]{0:T(1024)}, u32[]{:S(2)}) copy-start(f32[16384]{0:T(1024)} %mul.548) | copy-start | bytes 196612
  59.6 3.3 %copy-start.16 = (f32[16384]{0:T(1024)S(1)}, f32[16384]{0:T(1024)}, u32[]{:S(2)}) copy-start(f32[16384]{0:T(1024)} %mul.617) | copy-start | bytes 196612
  59.6 3.3 %copy-start.17 = (f32[16384]{0:T(1024)S(1)}, f32[16384]{0:T(1024)}, u32[]{:S(2)}) copy-start(f32[16384]{0:T(1024)} %mul.614) | copy-start | bytes 196612
  59.7 3.3 %copy-start.18 = (f32[16384]{0:T(1024)S(1)}, f32[16384]{0:T(1024)}, u32[]{:S(2)}) copy-start(f32[16384]{0:T(1024)} %mul.611) | copy-start | bytes 196612
  59.7 3.3 %copy-start.19 = (f32[16384]{0:T(1024)S(1)}, f32[16384]{0:T(1024)}, u32[]{:S(2)}) copy-start(f32[16384]{0:T(1024)} %mul.608) | copy-start | bytes 196612
  59.7 3.3 %copy-start.20 = (f32[16384]{0:T(1024)S(1)}, f32[16384]{0:T(1024)}, u32[]{:S(2)}) copy-start(f32[16384]{0:T(1024)} %mul.605) | copy-start | bytes 196612
  59.7 3.3 %copy-start.21 = (f32[16384]{0:T(1024)S(1)}, f32[16384]{0:T(1024)}, u32[]{:S(2)}) copy-start(f32[16384]{0:T(1024)} %mul.602) | copy-start | bytes 196612
  59.7 3.3 %copy-start.22 = (f32[16384]{0:T(1024)S(1)}, f32[16384]{0:T(1024)}, u32[]{:S(2)}) copy-start(f32[16384]{0:T(1024)} %mul.599) | copy-start | bytes 196612
  59.7 3.3 %copy-start.23 = (f32[16384]{0:T(1024)S(1)}, f32[16384]{0:T(1024)}, u32[]{:S(2)}) copy-start(f32[16384]{0:T(1024)} %mul.596) | copy-start | bytes 196612
  59.7 3.3 %copy-start.24 = (f32[16384]{0:T(1024)S(1)}, f32[16384]{0:T(1024)}, u32[]{:S(2)}) copy-start(f32[16384]{0:T(1024)} %mul.593) | copy-start | bytes 196612
  59.7 3.3 %copy-start.25 = (f32[16384]{0:T(1024)S(1)}, f32[16384]{0:T(1024)}, u32[]{:S(2)}) copy-start(f32[16384]{0:T(1024)} %mul.590) | copy-start | bytes 196612
  59.7 3.3 %copy-start.26 = (f32[16384]{0:T(1024)S(1)}, f32[16384]{0:T(1024)}, u32[]{:S(2)}) copy-start(f32[16384]{0:T(1024)} %mul.587) | copy-start | bytes 196612
  59.7 3.3 %copy-start.27 = (f32[16384]{0:T(1024)S(1)}, f32[16384]{0:T(1024)}, u32[]{:S(2)}) copy-start(f32[16384]{0:T(1024)} %mul.584) | copy-start | bytes 196612
  59.8 3.3 %copy-start.28 = (f32[16384]{0:T(1024)S(1)}, f32[16384]{0:T(1024)}, u32[]{:S(2)}) copy-start(f32[16384]{0:T(1024)} %mul.581) | copy-start | bytes 196612
  59.8 3.3 %copy-start.29 = (f32[16384]{0:T(1024)S(1)}, f32[16384]{0:T(1024)}, u32[]{:S(2)}) copy-start(f32[16384]{0:T(1024)} %mul.578) | copy-start | bytes 196612
  59.8 3.3 %copy-start.30 = (f32[16384]{0:T(1024)S(1)}, f32[16384]{0:T(1024)}, u32[]{:S(2)}) copy-start(f32[16384]{0:T(1024)} %mul.575) | copy-start | bytes 196612
  59.8 3.3 %copy-start.31 = (f32[16384]{0:T(1024)S(1)}, f32[16384]{0:T(1024)}, u32[]{:S(2)}) copy-start(f32[16384]{0:T(1024)} %mul.572) | copy-start | bytes 196612
  59.8 3.3 %copy-start.32 = (f32[16384]{0:T(1024)S(1)}, f32[16384]{0:T(1024)}, u32[]{:S(2)}) copy-start(f32[16384]{0:T(1024)} %mul.569) | copy-start | bytes 196612
  59.8 3.3 %copy-start.33 = (f32[16384]{0:T(1024)S(1)}, f32[16384]{0:T(1024)}, u32[]{:S(2)}) copy-start(f32[16384]{0:T(1024)} %mul.566) | copy-start | bytes 196612
  81.0 4.6 %copy-start.44 = (bf16[256,64]{0,1:T(8,128)(2,1)S(1)}, bf16[256,64]{0,1:T(8,128)(2,1)}, u32[]{:S(2)}) copy-start(bf16[256,64]{0,1:T(8,128)(2,1)} %param.10) | copy-start | bytes 98308
  89.0 12.2 %copy-start.7 = (f32[8192,64]{0,1:T(8,128)S(1)}, f32[8192,64]{0,1:T(8,128)}, u32[]{:S(2)}) copy-start(f32[8192,64]{0,1:T(8,128)} %fusion.5) | copy-start | bytes 6291460
  90.7 10.5 %copy-start.5 = (f32[32,256,64]{1,2,0:T(8,128)S(1)}, f32[32,256,64]{1,2,0:T(8,128)}, u32[]{:S(2)}) copy-start(f32[32,256,64]{1,2,0:T(8,128)} %copy.44) | copy-start | bytes 6291460
  117.0 13.4 %copy-start.4 = (bf16[2,16,16384]{2,1,0:T(8,128)(2,1)}, bf16[2,16,16384]{2,1,0:T(8,128)(2,1)S(1)}, u32[]{:S(2)}) copy-start(bf16[2,16,16384]{2,1,0:T(8,128)(2,1)S(1)} %reshape.72) | copy-start | bytes 3145732
  117.1 3.7 %collective-permute-start.7 = (bf16[2,16,64]{2,1,0:T(8,128)(2,1)S(1)}, bf16[2,16,64]{2,1,0:T(8,128)(2,1)S(1)}, u32[]{:S(2)}, u32[]{:S(2)}) collective-permute-start(bf16[2,16,64]{2,1,0:T(8,128)(2,1)S(1)} %get-tuple-element.17), channel_id=1, source_target_pairs={{8,0},{16,8},{24,16},{0,24},{9,1},{17,9},{25,17},{1,25},{10,2},{18... | collective-permute-start | bytes 12296 | tf_op jit(solution)/shard_map/ppermute | solution.py:16
  118.6 4.5 %collective-permute-start.6 = (bf16[2,16,64]{2,1,0:T(8,128)(2,1)S(1)}, bf16[2,16,64]{2,1,0:T(8,128)(2,1)S(1)}, u32[]{:S(2)}, u32[]{:S(2)}) collective-permute-start(bf16[2,16,64]{2,1,0:T(8,128)(2,1)S(1)} %get-tuple-element.18), channel_id=1, source_target_pairs={{0,8},{8,16},{16,24},{24,0},{1,9},{9,17},{17,25},{25,1},{2,10},{10... | collective-permute-start | bytes 12296 | tf_op jit(solution)/shard_map/ppermute | solution.py:15
  124.5 4.4 %collective-permute-start.9 = (bf16[2,1,16512]{2,1,0:T(2,128)(2,1)S(1)}, bf16[2,1,16512]{2,1,0:T(2,128)(2,1)S(1)}, u32[]{:S(2)}, u32[]{:S(2)}) collective-permute-start(bf16[2,1,16512]{2,1,0:T(2,128)(2,1)S(1)} %get-tuple-element.13), channel_id=1, source_target_pairs={{4,0},{5,1},{6,2},{7,3},{12,8},{13,9},{14,10},{15,11},{20,16},{21,... | collective-permute-start | bytes 198152 | tf_op jit(solution)/shard_map/ppermute | solution.py:16
  125.8 4.0 %collective-permute-start.8 = (bf16[2,1,16512]{2,1,0:T(2,128)(2,1)S(1)}, bf16[2,1,16512]{2,1,0:T(2,128)(2,1)S(1)}, u32[]{:S(2)}, u32[]{:S(2)}) collective-permute-start(bf16[2,1,16512]{2,1,0:T(2,128)(2,1)S(1)} %get-tuple-element.14), channel_id=1, source_target_pairs={{0,4},{1,5},{2,6},{3,7},{8,12},{9,13},{10,14},{11,15},{16,20},{17,... | collective-permute-start | bytes 198152 | tf_op jit(solution)/shard_map/ppermute | solution.py:15
  131.7 23.0 %collective-permute-start.10 = (bf16[1,18,16512]{2,1,0:T(8,128)(2,1)}, bf16[1,18,16512]{2,1,0:T(8,128)(2,1)}, u32[]{:S(2)}, u32[]{:S(2)}) collective-permute-start(bf16[1,18,16512]{2,1,0:T(8,128)(2,1)} %get-tuple-element.5), channel_id=1, source_target_pairs={{1,0},{2,1},{3,2},{5,4},{6,5},{7,6},{9,8},{10,9},{11,10},{13,12},{... | collective-permute-start | bytes 1783304 | tf_op jit(solution)/shard_map/ppermute | solution.py:16
  133.0 22.9 %collective-permute-start.11 = (bf16[1,18,16512]{2,1,0:T(8,128)(2,1)}, bf16[1,18,16512]{2,1,0:T(8,128)(2,1)}, u32[]{:S(2)}, u32[]{:S(2)}) collective-permute-start(bf16[1,18,16512]{2,1,0:T(8,128)(2,1)} %get-tuple-element.6), channel_id=1, source_target_pairs={{0,1},{1,2},{2,3},{4,5},{5,6},{6,7},{8,9},{9,10},{10,11},{12,13},{... | collective-permute-start | bytes 1783304 | tf_op jit(solution)/shard_map/ppermute | solution.py:15
  141.5 93.2 %all-reduce.2.cloned.1.call-start = ((), (), s32[]{:S(2)}) async-start(), calls=%async_computation.4 | async-start | bytes 524288 | tf_op jit(solution)/shard_map/psum | solution.py:100
  191.0 45.5 %copy-start.1 = (bf16[64,256]{1,0:T(8,128)(2,1)S(1)}, bf16[64,256]{1,0:T(8,128)(2,1)}, u32[]{:S(2)}) copy-start(bf16[64,256]{1,0:T(8,128)(2,1)} %param.9) | copy-start | bytes 98308
  (13 other events, 34.5 us)
Sparse Core Ops, SparseCore 0:
  24.6 27.1 reduce-scatter.2
  141.6 23.6 reduce-scatter.4
  179.7 54.9 all-reduce.1
where the time goes:
time: 244 us; the launch traced here: 243 us
  local copies, waits for them, and re-layouts  62.6 us (26%)
  other arithmetic  51.6 us (21%)
  waiting for transfers between devices  43.3 us (18%)
  starting transfers between devices  26.4 us (11%)
  matrix products  25.6 us (10%)
  blocking collectives  18.8 us (8%)
  between operations  14.7 us (6%)
    psum x1, waiting for transfers between devices, sum_gradients(): lax.psum(local_grads.astype(jnp.bfloat16), ('gy', 'gz')).astype(jnp.float32)  22.1 us
    convert_element_type x1, other arithmetic, per_device(): (grad_local + spectral_grad.reshape(planes, y_cells, merged)).astype(jnp....  21.6 us
    all_gather x2, blocking collectives, share_inverse(): segment = lax.all_gather(modes_share, 'gx', axis=0, tiled=True)  18.8 us
    mul x27, local copies, waits for them, and re-layouts, depthwise(): running = running + cut.astype(jnp.float32) * jnp.tile(tap_gain, x_cells)  18.6 us
    ppermute x6, starting transfers between devices, padded_2(): before = lax.ppermute(last, axis, up)  15.6 us
    convert_element_type x1, other arithmetic, per_device(): depthwise(padded, depth_weight, False, x_cells, channels)  14.8 us
    ppermute x6, waiting for transfers between devices, padded_2(): after = lax.ppermute(leading, axis, down)  11.2 us
    ppermute x6, starting transfers between devices, padded_2(): after = lax.ppermute(leading, axis, down)  10.7 us
  transfers between devices with their start and end apart: 15, of which 8 were waited for; matrix products, arithmetic and copies ran while one was open for 43% of the time, Pallas kernels for 0%

commit v1 on v0

--- a/solution.py
+++ b/solution.py
@@ -3,6 +3,24 @@
 import jax.numpy as jnp
 from jax import lax
 from jax.sharding import PartitionSpec as P
+
+
+def gather_around(value, axis, dim):
+    ways, here, turn = (lax.axis_size(axis), lax.axis_index(axis), value.shape[dim])
+    lengths = [n * ways if d == dim else n for d, n in enumerate(value.shape)]
+    full = lax.dynamic_update_slice_in_dim(
+        jnp.zeros(lengths, value.dtype), value, here * turn, axis=dim
+    )
+    going_up = going_down = value
+    for far in range(1, ways // 2 + 1):
+        going_up = lax.ppermute(going_up, axis, [(d, (d + 1) % ways) for d in range(ways)])
+        full = lax.dynamic_update_slice_in_dim(full, going_up, (here - far) % ways * turn, axis=dim)
+        if 2 * far < ways:
+            going_down = lax.ppermute(going_down, axis, [(d, (d - 1) % ways) for d in range(ways)])
+            full = lax.dynamic_update_slice_in_dim(
+                full, going_down, (here + far) % ways * turn, axis=dim
+            )
+    return full
 
 
 def padded_2(value, sides, width, wrap):
@@ -81,7 +99,7 @@
 
 
 def share_inverse(modes_share, cos_table, sin_table, channels):
-    segment = lax.all_gather(modes_share, "gx", axis=0, tiled=True)
+    segment = gather_around(modes_share, "gx", 0)
     running = jnp.einsum(
         "krc,xk->rxc", segment[:, :, :channels], cos_table, preferred_element_type=jnp.float32
     )

time: 244 us -> 267 us (1.094)
  waiting for transfers between devices: 43.3 us -> 77.2 us
  blocking collectives: 18.8 us -> 0 us
  starting transfers between devices: 26.4 us -> 33.4 us
    psum x1, waiting for transfers between devices: 22.1 us -> 48.3 us  [sum_gradients(): lax.psum(local_grads.astype(jnp.bfloat16), ('gy', 'gz')).astype(jnp.float32)]
    all_gather x2 -> x0, blocking collectives: 18.8 us -> none  [share_inverse(): segment = lax.all_gather(modes_share, 'gx', axis=0, tiled=True)]
    reduce_scatter x2, waiting for transfers between devices: 5.44 us -> 14.8 us  [share_terms(): lax.psum_scatter(jnp.concatenate([real_part, imag_part], axis=2), 'gx', s...]
    ppermute x0 -> x6, waiting for transfers between devices: none -> 7.23 us  [the longest x4 6.37 us: gather_around(): lax.ppermute(going_up, axis, [(d, (d + 1) % ways) for d in range(ways)])]
    mul x27, local copies, waits for them, and re-layouts: 18.6 us -> 11.5 us  [depthwise(): running = running + cut.astype(jnp.float32) * jnp.tile(tap_gain, x_cells)]
    ppermute x0 -> x6, starting transfers between devices: none -> 6.43 us  [the longest x2 3.82 us: gather_around(): lax.ppermute(going_down, axis, [(d, (d - 1) % ways) for d in range(ways)])]
    ppermute x6, waiting for transfers between devices: 11.2 us -> 5.88 us  [padded_2(): after = lax.ppermute(leading, axis, down)]
    dynamic_update_slice x0 -> x8, local copies, waits for them, and re-layouts: none -> 5.28 us  [the longest x4 3.03 us: gather_around(): lax.dynamic_update_slice_in_dim(full, going_up, (here - far) % ways * tur...]
  transfers between devices with their start and end apart: 15 -> 21, of which waited for: 8 -> 8; matrix products, arithmetic and copies ran while one was open for 43% -> 28% of each run, Pallas kernels for 0% -> 0%
where the time goes in v1:
time: 267 us; the launch traced here: 266 us
  waiting for transfers between devices  77.2 us (29%)
  local copies, waits for them, and re-layouts  61.6 us (23%)
  other arithmetic  51.9 us (19%)
  starting transfers between devices  33.4 us (13%)
  matrix products  27.2 us (10%)
  between operations  14.9 us (6%)
    psum x1, waiting for transfers between devices, sum_gradients(): lax.psum(local_grads.astype(jnp.bfloat16), ('gy', 'gz')).astype(jnp.float32)  48.3 us
    convert_element_type x1, other arithmetic, per_device(): (grad_local + spectral_grad.reshape(planes, y_cells, merged)).astype(jnp....  21.2 us
    ppermute x6, starting transfers between devices, padded_2(): before = lax.ppermute(last, axis, up)  17.6 us
    reduce_scatter x2, waiting for transfers between devices, share_terms(): lax.psum_scatter(jnp.concatenate([real_part, imag_part], axis=2), 'gx', s...  14.8 us
    convert_element_type x1, other arithmetic, per_device(): depthwise(padded, depth_weight, False, x_cells, channels)  14.7 us
    mul x27, local copies, waits for them, and re-layouts, depthwise(): running = running + cut.astype(jnp.float32) * jnp.tile(tap_gain, x_cells)  11.5 us
    ppermute x6, starting transfers between devices, padded_2(): after = lax.ppermute(leading, axis, down)  9.24 us
    concatenate x4, other arithmetic, padded_2(): value = jnp.concatenate([before, value, after], axis=dim)  7.92 us
  transfers between devices with their start and end apart: 21, of which 8 were waited for; matrix products, arithmetic and copies ran while one was open for 28% of the time, Pallas kernels for 0%

profile of v1, /device:TPU:0, one launch (start us, length us, event | category | flops | bytes accessed | tf_op | source)
XLA Modules:
  0.0 266.3 jit_solution(9782478810152942613)
XLA Ops:
  8.0 2.9 %collective-permute-start = (bf16[2,16,64]{2,1,0:T(8,128)(2,1)S(1)}, bf16[2,16,64]{2,1,0:T(8,128)(2,1)S(1)}, u32[]{:S(2)}, u32[]{:S(2)}) collective-permute-start(bf16[2,16,64]{2,1,0:T(8,128)(2,1)S(1)} %get-tuple-element.22), channel_id=1, source_target_pairs={{0,8},{8,16},{16,24},{24,0},{1,9},{9,17},{17,25},{25,1},{2,10},{10... | collective-permute-start | bytes 12296 | tf_op jit(solution)/shard_map/ppermute | solution.py:33
  12.0 3.0 %reshape.69 = bf16[32,256,64]{2,1,0:T(8,128)(2,1)S(1)} reshape(bf16[2,16,16384]{2,1,0:T(8,128)(2,1)} %param.7) | data formatting | bytes 2097152 | tf_op jit(solution)/shard_map/reshape | solution.py:145
  15.0 1.4 fusion.48
  16.4 1.3 fusion.51
  17.7 2.9 %concatenate.105 = bf16[2,16,16512]{2,1,0:T(8,128)(2,1)S(1)} concatenate(bf16[2,16,64]{2,1,0:T(8,128)(2,1)S(1)} %collective-permute-done, bf16[2,16,16384]{2,1,0:T(8,128)(2,1)} %param.7, bf16[2,16,64]{2,1,0:T(8,128)(2,1)S(1)} %collective-permute-done.1), dimensions={2} | concatenate | bytes 2113536 | tf_op jit(solution)/shard_map/concatenate | solution.py:35
  21.5 1.3 collective-permute-start.3
  22.8 3.0 %collective-permute-start.2 = (bf16[2,1,16512]{2,1,0:T(2,128)(2,1)}, bf16[2,1,16512]{2,1,0:T(2,128)(2,1)S(1)}, u32[]{:S(2)}, u32[]{:S(2)}) collective-permute-start(bf16[2,1,16512]{2,1,0:T(2,128)(2,1)} %get-tuple-element.17), channel_id=1, source_target_pairs={{0,4},{1,5},{2,6},{3,7},{8,12},{9,13},{10,14},{11,15},{16,20},{17,... | collective-permute-start | bytes 198152 | tf_op jit(solution)/shard_map/ppermute | solution.py:33
  27.0 3.3 %reshape.101 = f32[32,256,64]{2,1,0:T(8,128)} reshape(bf16[2,16,16384]{2,1,0:T(8,128)(2,1)S(1)} %copy-done.16) | data formatting | bytes 3145728 | tf_op jit(solution)/shard_map/convert_element_type | solution.py:158
  30.3 3.8 %copy.31 = f32[32,256,64]{1,2,0:T(8,128)} copy(f32[32,256,64]{2,1,0:T(8,128)} %reshape.101) | data formatting | bytes 4194304 | tf_op jit(solution)/shard_map/convert_element_type | solution.py:158
  34.9 1.2 fusion.95
  36.2 4.8 %collective-permute-start.4 = (bf16[1,18,16512]{2,1,0:T(8,128)(2,1)}, bf16[1,18,16512]{2,1,0:T(8,128)(2,1)}, u32[]{:S(2)}, u32[]{:S(2)}) collective-permute-start(bf16[1,18,16512]{2,1,0:T(8,128)(2,1)} %get-tuple-element.9), channel_id=1, source_target_pairs={{0,1},{1,2},{2,3},{4,5},{5,6},{6,7},{8,9},{9,10},{10,11},{12,13},{... | collective-permute-start | bytes 1783304 | tf_op jit(solution)/shard_map/ppermute | solution.py:33
  41.0 1.5 collective-permute-start.5
  56.9 5.0 %collective-permute-done.5 = bf16[1,18,16512]{2,1,0:T(8,128)(2,1)} collective-permute-done((bf16[1,18,16512]{2,1,0:T(8,128)(2,1)}, bf16[1,18,16512]{2,1,0:T(8,128)(2,1)}, u32[]{:S(2)}, u32[]{:S(2)}) %collective-permute-start.5) | collective-permute-done | bytes 594464 | tf_op jit(solution)/shard_map/ppermute | solution.py:34
  61.9 2.8 %maximum_maximum_fusion = (bf16[3,18,16512]{2,1,0:T(8,128)(2,1)S(1)}, bf16[3,18,16512]{2,1,0:T(8,128)(2,1)S(1)}) fusion(bf16[2,1,16512]{2,1,0:T(2,128)(2,1)S(1)} %collective-permute-done.3, bf16[2,16,16512]{2,1,0:T(8,128)(2,1)S(1)} %concatenate.105, bf16[2,1,16512]{2,1,0:T(2,128)(2,1)S(1)} %collective-permute-done.2, ...), kind=kLoop, calls=%fused_computation.12 | loop fusion | flops 14266368 | bytes 5944320 | tf_op jit(solution)/shard_map/concatenate | solution.py:35
  65.0 14.7 %add_convert_fusion.1 = bf16[2,16,16384]{2,1,0:T(8,128)(2,1)} fusion(bf16[2,16,16384]{2,1,0:T(8,128)(2,1)S(1)} %copy-done.3, bf16[2,16,16512]{2,1,0:T(8,128)(2,1)S(1)} %concatenate.105, bf16[2,1,16512]{2,1,0:T(2,128)(2,1)S(1)} %collective-permute-done.3, bf16[2,1,16512]{2,1,0:T(2,128)(2,1)S(1)} %collective-permute-done.2, ...), kind=kLoop, calls=%fused_computation.35 | loop fusion | flops 55050240 | bytes 23938048 | tf_op jit(solution)/shard_map/convert_element_type | solution.py:137
  79.7 3.0 %reshape.67 = bf16[8192,64]{1,0:T(8,128)(2,1)S(1)} reshape(bf16[2,16,16384]{2,1,0:T(8,128)(2,1)} %add_convert_fusion.1) | data formatting | bytes 2097152 | tf_op jit(solution)/shard_map/reshape | solution.py:138
  84.0 3.3 %copy-done.2 = f32[8192,256]{1,0:T(8,128)} copy-done((f32[8192,256]{1,0:T(8,128)}, f32[8192,256]{1,0:T(8,128)S(1)}, u32[]{:S(2)}) %copy-start.2) | copy-done | bytes 8388632
  87.3 3.3 %fusion.5 = f32[8192,64]{0,1:T(8,128)} fusion(bf16[256,64]{0,1:T(8,128)(2,1)S(1)} %copy-done.47, f32[8192,256]{1,0:T(8,128)S(1)} %fusion.100), kind=kOutput, calls=%fused_computation.10 | convolution fusion | flops 278921216 | bytes 10518528 | tf_op jit(solution)/shard_map/dot_general | solution.py:141
  92.5 2.3 collective-permute-start.7
  95.0 2.1 collective-permute-done.6
  98.1 4.2 %collective-permute-done.8 = bf16[8,32,128]{2,1,0:T(8,128)(2,1)S(1)} collective-permute-done((bf16[8,32,128]{2,1,0:T(8,128)(2,1)S(1)}, bf16[8,32,128]{2,1,0:T(8,128)(2,1)S(1)}, u32[]{:S(2)}, u32[]{:S(2)}) %collective-permute-start.8) | collective-permute-done | bytes 65568 | tf_op jit(solution)/shard_map/ppermute | solution.py:16
  103.2 3.8 %fusion.11 = (bf16[32,256,64]{1,2,0:T(8,128)(2,1)S(1)}, bf16[32,256,64]{1,2,0:T(8,128)(2,1)}) fusion(f32[32,256,64]{1,2,0:T(8,128)S(1)} %copy-done.5, f32[256,32,64]{0,2,1:T(8,128)S(1)} %fusion.28, bf16[32,32,128]{2,0,1:T(8,128)(2,1)S(1)} %copy_dynamic-update-slice_fusion, f32[32]{0:T(128)S(1)} %fusion.67, s32[256]{0:T(256)S(1)} %iota_add_fusion, ...), kind=kOutput, calls=%fused_computation.29 | convolution fusion | flops 41041920 | bytes 8651904 | tf_op jit(solution)/shard_map/krc,xk->rxc/dot_general | solution.py:103
  107.0 1.4 fusion.53
  108.5 7.9 %convolution_convert_fusion = bf16[8192,64]{0,1:T(8,128)(2,1)S(1)} fusion(bf16[64,256]{1,0:T(8,128)(2,1)S(1)} %copy-done, bf16[8192,64]{0,1:T(8,128)(2,1)S(1)} %bitcast.128, bf16[256,64]{0,1:T(8,128)(2,1)} %param.10, f32[8192,256]{1,0:T(8,128)} %copy-done.2), kind=kOutput, calls=%fused_computation.3 | convolution fusion | flops 558366720 | bytes 10551296 | tf_op jit(solution)/shard_map/dot_general | solution.py:166
  116.4 1.8 copy.33
  118.1 2.9 %reshape.72 = bf16[2,16,16384]{2,1,0:T(8,128)(2,1)S(1)} reshape(bf16[8192,64]{1,0:T(8,128)(2,1)} %copy.33) | data formatting | bytes 2097152 | tf_op jit(solution)/shard_map/reshape | solution.py:169
  121.2 2.9 %collective-permute-start.10 = (bf16[2,16,64]{2,1,0:T(8,128)(2,1)S(1)}, bf16[2,16,64]{2,1,0:T(8,128)(2,1)S(1)}, u32[]{:S(2)}, u32[]{:S(2)}) collective-permute-start(bf16[2,16,64]{2,1,0:T(8,128)(2,1)S(1)} %get-tuple-element.19), channel_id=1, source_target_pairs={{8,0},{16,8},{24,16},{0,24},{9,1},{17,9},{25,17},{1,25},{10,2},{18... | collective-permute-start | bytes 12296 | tf_op jit(solution)/shard_map/ppermute | solution.py:34
  124.1 1.4 fusion.56
  125.6 1.8 copy.30
  127.3 3.7 %reshape.70 = bf16[2,16,16384]{2,1,0:T(8,128)(2,1)} reshape(bf16[32,256,64]{2,1,0:T(8,128)(2,1)} %copy.30) | data formatting | bytes 2097152 | tf_op jit(solution)/shard_map/reshape | solution.py:156
  132.4 1.3 collective-permute-start.11
  133.7 1.3 collective-permute-start.12
  138.5 1.3 collective-permute-start.13
  139.8 5.5 %collective-permute-start.14 = (bf16[1,18,16512]{2,1,0:T(8,128)(2,1)S(1)}, bf16[1,18,16512]{2,1,0:T(8,128)(2,1)}, u32[]{:S(2)}, u32[]{:S(2)}) collective-permute-start(bf16[1,18,16512]{2,1,0:T(8,128)(2,1)S(1)} %get-tuple-element.8), channel_id=1, source_target_pairs={{0,1},{1,2},{2,3},{4,5},{5,6},{6,7},{8,9},{9,10},{10,11},{12,13},{... | collective-permute-start | bytes 1783304 | tf_op jit(solution)/shard_map/ppermute | solution.py:33
  145.3 14.8 %reduce-scatter.5.cloned.1.call-done = f32[8,32,128]{2,0,1:T(8,128)} async-done(((f32[32,32,128]{2,0,1:T(8,128)}), f32[8,32,128]{2,0,1:T(8,128)}) %reduce-scatter.5.cloned.1.call-update) | async-done | bytes 131088 | tf_op jit(solution)/shard_map/reduce_scatter | solution.py:96
  162.7 1.4 collective-permute-start.15
  166.3 3.9 %pad_maximum_fusion.1 = (bf16[3,18,16512]{2,1,0:T(8,128)(2,1)S(1)}, bf16[3,18,16512]{2,1,0:T(8,128)(2,1)}) fusion(bf16[1,18,16512]{2,1,0:T(8,128)(2,1)} %copy-done.17, bf16[2,1,16512]{2,1,0:T(2,128)(2,1)} %copy-done.15, bf16[2,16,16512]{2,1,0:T(8,128)(2,1)S(1)} %concatenate.117, bf16[2,1,16512]{2,1,0:T(2,128)(2,1)} %copy-done.14, ...), kind=kLoop, calls=%fused_computation.14 | loop fusion | flops 14266368 | bytes 5944320 | tf_op jit(solution)/shard_map/concatenate | solution.py:35
  170.2 1.5 collective-permute-start.16
  172.3 48.3 %all-reduce.2.cloned.1.call-done = bf16[2,8,64,64]{3,2,1,0:T(8,128)(2,1)} async-done(((bf16[2,8,64,64]{3,2,1,0:T(8,128)(2,1)}), bf16[2,8,64,64]{3,2,1,0:T(8,128)(2,1)}) %all-reduce.2.cloned.1.call-update) | async-done | bytes 131088 | tf_op jit(solution)/shard_map/psum | solution.py:118
  220.6 1.8 convert_element_type.381
  222.3 1.5 constant_dynamic-update-slice_fusion.2
  223.8 1.5 constant_dynamic-update-slice_fusion.1
  225.3 1.5 constant_dynamic-update-slice_fusion
  226.8 2.0 fusion.25
  228.8 2.0 add_bitcast_fusion
  230.8 3.8 %copy.36 = f32[32,256,64]{2,1,0:T(8,128)} copy(f32[32,256,64]{1,2,0:T(8,128)} %add_bitcast_fusion) | data formatting | bytes 4194304 | tf_op jit(solution)/shard_map/add | solution.py:106
  234.6 3.9 %reshape.73 = f32[2,16,16384]{2,1,0:T(8,128)} reshape(f32[32,256,64]{2,1,0:T(8,128)} %copy.36) | data formatting | bytes 4194304 | tf_op jit(solution)/shard_map/reshape | solution.py:179
  238.5 21.2 %add_convert_fusion = bf16[2,16,16384]{2,1,0:T(8,128)(2,1)} fusion(f32[2,16,16384]{2,1,0:T(8,128)} %reshape.73, bf16[2,16,16384]{2,1,0:T(8,128)(2,1)} %copy-done.4, bf16[2,16,16512]{2,1,0:T(8,128)(2,1)S(1)} %concatenate.117, bf16[2,1,16512]{2,1,0:T(2,128)(2,1)} %copy-done.14, bf16[2,1,16512]{2,1,0:T(2,128)(2,1)} %copy-done.15, ...), kind=kLoop, calls=%fused_computation.31 | loop fusion | flops 55574528 | bytes 26035200 | tf_op jit(solution)/shard_map/convert_element_type | solution.py:179
  (209 shorter events, 33.9 us)
Async XLA Ops:
  7.2 75.6 %copy-start = (bf16[64,256]{1,0:T(8,128)(2,1)S(1)}, bf16[64,256]{1,0:T(8,128)(2,1)}, u32[]{:S(2)}) copy-start(bf16[64,256]{1,0:T(8,128)(2,1)} %param.9) | copy-start | bytes 98308
  7.2 83.5 %reduce-scatter.3.cloned.1.call-start = ((), (), s32[]{:S(2)}) async-start(), calls=%async_computation.2 | async-start | bytes 655360 | tf_op jit(solution)/shard_map/reduce_scatter | solution.py:96
  8.0 9.7 %collective-permute-start = (bf16[2,16,64]{2,1,0:T(8,128)(2,1)S(1)}, bf16[2,16,64]{2,1,0:T(8,128)(2,1)S(1)}, u32[]{:S(2)}, u32[]{:S(2)}) collective-permute-start(bf16[2,16,64]{2,1,0:T(8,128)(2,1)S(1)} %get-tuple-element.22), channel_id=1, source_target_pairs={{0,8},{8,16},{16,24},{24,0},{1,9},{9,17},{17,25},{25,1},{2,10},{10... | collective-permute-start | bytes 12296 | tf_op jit(solution)/shard_map/ppermute | solution.py:33
  11.0 6.8 %collective-permute-start.1 = (bf16[2,16,64]{2,1,0:T(8,128)(2,1)S(1)}, bf16[2,16,64]{2,1,0:T(8,128)(2,1)S(1)}, u32[]{:S(2)}, u32[]{:S(2)}) collective-permute-start(bf16[2,16,64]{2,1,0:T(8,128)(2,1)S(1)} %get-tuple-element.21), channel_id=1, source_target_pairs={{8,0},{16,8},{24,16},{0,24},{9,1},{17,9},{25,17},{1,25},{10,2},{18... | collective-permute-start | bytes 12296 | tf_op jit(solution)/shard_map/ppermute | solution.py:34
  17.7 9.3 %copy-start.16 = (bf16[2,16,16384]{2,1,0:T(8,128)(2,1)S(1)}, bf16[2,16,16384]{2,1,0:T(8,128)(2,1)}, u32[]{:S(2)}) copy-start(bf16[2,16,16384]{2,1,0:T(8,128)(2,1)} %param.13) | copy-start | bytes 3145732
  21.5 12.8 %collective-permute-start.3 = (bf16[2,1,16512]{2,1,0:T(2,128)(2,1)}, bf16[2,1,16512]{2,1,0:T(2,128)(2,1)S(1)}, u32[]{:S(2)}, u32[]{:S(2)}) collective-permute-start(bf16[2,1,16512]{2,1,0:T(2,128)(2,1)} %get-tuple-element.18), channel_id=1, source_target_pairs={{4,0},{5,1},{6,2},{7,3},{12,8},{13,9},{14,10},{15,11},{20,16},{21,... | collective-permute-start | bytes 198152 | tf_op jit(solution)/shard_map/ppermute | solution.py:34
  22.8 11.5 %collective-permute-start.2 = (bf16[2,1,16512]{2,1,0:T(2,128)(2,1)}, bf16[2,1,16512]{2,1,0:T(2,128)(2,1)S(1)}, u32[]{:S(2)}, u32[]{:S(2)}) collective-permute-start(bf16[2,1,16512]{2,1,0:T(2,128)(2,1)} %get-tuple-element.17), channel_id=1, source_target_pairs={{0,4},{1,5},{2,6},{3,7},{8,12},{9,13},{10,14},{11,15},{16,20},{17,... | collective-permute-start | bytes 198152 | tf_op jit(solution)/shard_map/ppermute | solution.py:33
  26.9 133.2 %reduce-scatter.5.cloned.1.call-start = ((), (), s32[]{:S(2)}) async-start(), calls=%async_computation.3 | async-start | bytes 655360 | tf_op jit(solution)/shard_map/reduce_scatter | solution.py:96
  36.2 20.7 %collective-permute-start.4 = (bf16[1,18,16512]{2,1,0:T(8,128)(2,1)}, bf16[1,18,16512]{2,1,0:T(8,128)(2,1)}, u32[]{:S(2)}, u32[]{:S(2)}) collective-permute-start(bf16[1,18,16512]{2,1,0:T(8,128)(2,1)} %get-tuple-element.9), channel_id=1, source_target_pairs={{0,1},{1,2},{2,3},{4,5},{5,6},{6,7},{8,9},{9,10},{10,11},{12,13},{... | collective-permute-start | bytes 1783304 | tf_op jit(solution)/shard_map/ppermute | solution.py:33
  41.0 20.9 %collective-permute-start.5 = (bf16[1,18,16512]{2,1,0:T(8,128)(2,1)}, bf16[1,18,16512]{2,1,0:T(8,128)(2,1)}, u32[]{:S(2)}, u32[]{:S(2)}) collective-permute-start(bf16[1,18,16512]{2,1,0:T(8,128)(2,1)} %get-tuple-element.10), channel_id=1, source_target_pairs={{1,0},{2,1},{3,2},{5,4},{6,5},{7,6},{9,8},{10,9},{11,10},{13,12},{... | collective-permute-start | bytes 1783304 | tf_op jit(solution)/shard_map/ppermute | solution.py:34
  42.7 22.0 %copy-start.18 = (f32[16384]{0:T(1024)}, f32[16384]{0:T(1024)S(1)}, u32[]{:S(2)}) copy-start(f32[16384]{0:T(1024)S(1)} %mul.634) | copy-start | bytes 196612
  42.9 21.8 %copy-start.19 = (f32[16384]{0:T(1024)}, f32[16384]{0:T(1024)S(1)}, u32[]{:S(2)}) copy-start(f32[16384]{0:T(1024)S(1)} %mul.631) | copy-start | bytes 196612
  43.0 21.7 %copy-start.20 = (f32[16384]{0:T(1024)}, f32[16384]{0:T(1024)S(1)}, u32[]{:S(2)}) copy-start(f32[16384]{0:T(1024)S(1)} %mul.628) | copy-start | bytes 196612
  43.1 21.6 %copy-start.21 = (f32[16384]{0:T(1024)}, f32[16384]{0:T(1024)S(1)}, u32[]{:S(2)}) copy-start(f32[16384]{0:T(1024)S(1)} %mul.625) | copy-start | bytes 196612
  43.2 21.5 %copy-start.22 = (f32[16384]{0:T(1024)}, f32[16384]{0:T(1024)S(1)}, u32[]{:S(2)}) copy-start(f32[16384]{0:T(1024)S(1)} %mul.622) | copy-start | bytes 196612
  43.3 21.4 %copy-start.23 = (f32[16384]{0:T(1024)}, f32[16384]{0:T(1024)S(1)}, u32[]{:S(2)}) copy-start(f32[16384]{0:T(1024)S(1)} %mul.619) | copy-start | bytes 196612
  43.4 21.3 %copy-start.24 = (f32[16384]{0:T(1024)}, f32[16384]{0:T(1024)S(1)}, u32[]{:S(2)}) copy-start(f32[16384]{0:T(1024)S(1)} %mul.616) | copy-start | bytes 196612
  43.5 21.2 %copy-start.25 = (f32[16384]{0:T(1024)}, f32[16384]{0:T(1024)S(1)}, u32[]{:S(2)}) copy-start(f32[16384]{0:T(1024)S(1)} %mul.613) | copy-start | bytes 196612
  43.7 21.1 %copy-start.26 = (f32[16384]{0:T(1024)}, f32[16384]{0:T(1024)S(1)}, u32[]{:S(2)}) copy-start(f32[16384]{0:T(1024)S(1)} %mul.610) | copy-start | bytes 196612
  43.8 21.0 %copy-start.27 = (f32[16384]{0:T(1024)}, f32[16384]{0:T(1024)S(1)}, u32[]{:S(2)}) copy-start(f32[16384]{0:T(1024)S(1)} %mul.607) | copy-start | bytes 196612
  43.9 20.9 %copy-start.28 = (f32[16384]{0:T(1024)}, f32[16384]{0:T(1024)S(1)}, u32[]{:S(2)}) copy-start(f32[16384]{0:T(1024)S(1)} %mul.604) | copy-start | bytes 196612
  55.8 9.0 %copy-start.3 = (bf16[2,16,16384]{2,1,0:T(8,128)(2,1)S(1)}, bf16[2,16,16384]{2,1,0:T(8,128)(2,1)}, u32[]{:S(2)}) copy-start(bf16[2,16,16384]{2,1,0:T(8,128)(2,1)} %param.7) | copy-start | bytes 3145732
  55.8 9.0 %copy-start.29 = (f32[16384]{0:T(1024)S(1)}, f32[16384]{0:T(1024)}, u32[]{:S(2)}) copy-start(f32[16384]{0:T(1024)} %mul.601) | copy-start | bytes 196612
  55.8 9.0 %copy-start.30 = (f32[16384]{0:T(1024)S(1)}, f32[16384]{0:T(1024)}, u32[]{:S(2)}) copy-start(f32[16384]{0:T(1024)} %mul.598) | copy-start | bytes 196612
  55.8 9.0 %copy-start.31 = (f32[16384]{0:T(1024)S(1)}, f32[16384]{0:T(1024)}, u32[]{:S(2)}) copy-start(f32[16384]{0:T(1024)} %mul.595) | copy-start | bytes 196612
  55.8 9.0 %copy-start.32 = (f32[16384]{0:T(1024)S(1)}, f32[16384]{0:T(1024)}, u32[]{:S(2)}) copy-start(f32[16384]{0:T(1024)} %mul.592) | copy-start | bytes 196612
  55.8 9.0 %copy-start.33 = (f32[16384]{0:T(1024)S(1)}, f32[16384]{0:T(1024)}, u32[]{:S(2)}) copy-start(f32[16384]{0:T(1024)} %mul.589) | copy-start | bytes 196612
  55.8 9.0 %copy-start.34 = (f32[16384]{0:T(1024)S(1)}, f32[16384]{0:T(1024)}, u32[]{:S(2)}) copy-start(f32[16384]{0:T(1024)} %mul.586) | copy-start | bytes 196612
  55.8 9.0 %copy-start.35 = (f32[16384]{0:T(1024)S(1)}, f32[16384]{0:T(1024)}, u32[]{:S(2)}) copy-start(f32[16384]{0:T(1024)} %mul.583) | copy-start | bytes 196612
  55.8 9.0 %copy-start.36 = (f32[16384]{0:T(1024)S(1)}, f32[16384]{0:T(1024)}, u32[]{:S(2)}) copy-start(f32[16384]{0:T(1024)} %mul.580) | copy-start | bytes 196612
  90.7 12.6 %copy-start.5 = (f32[32,256,64]{1,2,0:T(8,128)S(1)}, f32[32,256,64]{1,2,0:T(8,128)}, u32[]{:S(2)}) copy-start(f32[32,256,64]{1,2,0:T(8,128)} %copy.31) | copy-start | bytes 6291460
  91.7 11.5 %copy-start.44 = (bf16[8,32,128]{2,0,1:T(8,128)(2,1)}, bf16[8,32,128]{2,0,1:T(8,128)(2,1)S(1)}, u32[]{:S(2)}) copy-start(bf16[8,32,128]{2,0,1:T(8,128)(2,1)S(1)} %convert_element_type.341) | copy-start | bytes 196612
  91.9 5.2 %collective-permute-start.6 = (bf16[8,32,128]{2,1,0:T(8,128)(2,1)S(1)}, bf16[8,32,128]{2,1,0:T(8,128)(2,1)S(1)}, u32[]{:S(2)}, u32[]{:S(2)}) collective-permute-start(bf16[8,32,128]{2,1,0:T(8,128)(2,1)S(1)} %convolution_convert_fusion.1), channel_id=1, source_target_pairs={{0,8},{8,16},{16,24},{24,0},{1,9},{9,17},{17,25},{25,1},{2,10},{10... | collective-permute-start | bytes 196616 | tf_op jit(solution)/shard_map/ppermute | solution.py:16
  92.5 5.5 %collective-permute-start.7 = (bf16[8,32,128]{2,1,0:T(8,128)(2,1)S(1)}, bf16[8,32,128]{2,1,0:T(8,128)(2,1)S(1)}, u32[]{:S(2)}, u32[]{:S(2)}) collective-permute-start(bf16[8,32,128]{2,1,0:T(8,128)(2,1)S(1)} %convolution_convert_fusion.1), channel_id=1, source_target_pairs={{0,24},{8,0},{16,8},{24,16},{1,25},{9,1},{17,9},{25,17},{2,26},{10... | collective-permute-start | bytes 196616 | tf_op jit(solution)/shard_map/ppermute | solution.py:19
  97.1 5.2 %collective-permute-start.8 = (bf16[8,32,128]{2,1,0:T(8,128)(2,1)S(1)}, bf16[8,32,128]{2,1,0:T(8,128)(2,1)S(1)}, u32[]{:S(2)}, u32[]{:S(2)}) collective-permute-start(bf16[8,32,128]{2,1,0:T(8,128)(2,1)S(1)} %collective-permute-done.6), channel_id=1, source_target_pairs={{0,8},{8,16},{16,24},{24,0},{1,9},{9,17},{17,25},{25,1},{2,10},{10... | collective-permute-start | bytes 196616 | tf_op jit(solution)/shard_map/ppermute | solution.py:16
  121.1 9.9 %copy-start.4 = (bf16[2,16,16384]{2,1,0:T(8,128)(2,1)}, bf16[2,16,16384]{2,1,0:T(8,128)(2,1)S(1)}, u32[]{:S(2)}) copy-start(bf16[2,16,16384]{2,1,0:T(8,128)(2,1)S(1)} %reshape.72) | copy-start | bytes 3145732
  121.2 9.8 %collective-permute-start.9 = (bf16[2,16,64]{2,1,0:T(8,128)(2,1)S(1)}, bf16[2,16,64]{2,1,0:T(8,128)(2,1)S(1)}, u32[]{:S(2)}, u32[]{:S(2)}) collective-permute-start(bf16[2,16,64]{2,1,0:T(8,128)(2,1)S(1)} %get-tuple-element.20), channel_id=1, source_target_pairs={{0,8},{8,16},{16,24},{24,0},{1,9},{9,17},{17,25},{25,1},{2,10},{10... | collective-permute-start | bytes 12296 | tf_op jit(solution)/shard_map/ppermute | solution.py:33
  121.2 9.8 %collective-permute-start.10 = (bf16[2,16,64]{2,1,0:T(8,128)(2,1)S(1)}, bf16[2,16,64]{2,1,0:T(8,128)(2,1)S(1)}, u32[]{:S(2)}, u32[]{:S(2)}) collective-permute-start(bf16[2,16,64]{2,1,0:T(8,128)(2,1)S(1)} %get-tuple-element.19), channel_id=1, source_target_pairs={{8,0},{16,8},{24,16},{0,24},{9,1},{17,9},{25,17},{1,25},{10,2},{18... | collective-permute-start | bytes 12296 | tf_op jit(solution)/shard_map/ppermute | solution.py:34
  132.4 3.7 %collective-permute-start.11 = (bf16[2,1,16512]{2,1,0:T(2,128)(2,1)S(1)}, bf16[2,1,16512]{2,1,0:T(2,128)(2,1)S(1)}, u32[]{:S(2)}, u32[]{:S(2)}) collective-permute-start(bf16[2,1,16512]{2,1,0:T(2,128)(2,1)S(1)} %get-tuple-element.16), channel_id=1, source_target_pairs={{0,4},{1,5},{2,6},{3,7},{8,12},{9,13},{10,14},{11,15},{16,20},{17,... | collective-permute-start | bytes 198152 | tf_op jit(solution)/shard_map/ppermute | solution.py:33
  133.7 3.2 %collective-permute-start.12 = (bf16[2,1,16512]{2,1,0:T(2,128)(2,1)S(1)}, bf16[2,1,16512]{2,1,0:T(2,128)(2,1)S(1)}, u32[]{:S(2)}, u32[]{:S(2)}) collective-permute-start(bf16[2,1,16512]{2,1,0:T(2,128)(2,1)S(1)} %get-tuple-element.15), channel_id=1, source_target_pairs={{4,0},{5,1},{6,2},{7,3},{12,8},{13,9},{14,10},{15,11},{20,16},{21,... | collective-permute-start | bytes 198152 | tf_op jit(solution)/shard_map/ppermute | solution.py:34
  136.0 84.5 %all-reduce.2.cloned.1.call-start = ((), (), s32[]{:S(2)}) async-start(), calls=%async_computation.4 | async-start | bytes 524288 | tf_op jit(solution)/shard_map/psum | solution.py:118
  137.5 26.6 %copy-start.45 = (bf16[8,32,128]{2,0,1:T(8,128)(2,1)S(1)}, bf16[8,32,128]{2,0,1:T(8,128)(2,1)}, u32[]{:S(2)}) copy-start(bf16[8,32,128]{2,0,1:T(8,128)(2,1)} %copy-done.44) | copy-start | bytes 196612
  138.5 26.9 %collective-permute-start.13 = (bf16[1,18,16512]{2,1,0:T(8,128)(2,1)}, bf16[1,18,16512]{2,1,0:T(8,128)(2,1)S(1)}, u32[]{:S(2)}, u32[]{:S(2)}) collective-permute-start(bf16[1,18,16512]{2,1,0:T(8,128)(2,1)} %get-tuple-element.7), channel_id=1, source_target_pairs={{1,0},{2,1},{3,2},{5,4},{6,5},{7,6},{9,8},{10,9},{11,10},{13,12},{... | collective-permute-start | bytes 1783304 | tf_op jit(solution)/shard_map/ppermute | solution.py:34
  139.8 26.5 %collective-permute-start.14 = (bf16[1,18,16512]{2,1,0:T(8,128)(2,1)S(1)}, bf16[1,18,16512]{2,1,0:T(8,128)(2,1)}, u32[]{:S(2)}, u32[]{:S(2)}) collective-permute-start(bf16[1,18,16512]{2,1,0:T(8,128)(2,1)S(1)} %get-tuple-element.8), channel_id=1, source_target_pairs={{0,1},{1,2},{2,3},{4,5},{5,6},{6,7},{8,9},{9,10},{10,11},{12,13},{... | collective-permute-start | bytes 1783304 | tf_op jit(solution)/shard_map/ppermute | solution.py:33
  162.7 9.0 %collective-permute-start.15 = (bf16[8,32,128]{2,0,1:T(8,128)(2,1)}, bf16[8,32,128]{2,0,1:T(8,128)(2,1)}, u32[]{:S(2)}, u32[]{:S(2)}) collective-permute-start(bf16[8,32,128]{2,0,1:T(8,128)(2,1)} %get-tuple-element.4), channel_id=1, source_target_pairs={{0,8},{8,16},{16,24},{24,0},{1,9},{9,17},{17,25},{25,1},{2,10},{10... | collective-permute-start | bytes 196616 | tf_op jit(solution)/shard_map/ppermute | solution.py:16
  170.2 53.6 %collective-permute-start.16 = (bf16[8,32,128]{2,0,1:T(8,128)(2,1)}, bf16[8,32,128]{2,0,1:T(8,128)(2,1)}, u32[]{:S(2)}, u32[]{:S(2)}) collective-permute-start(bf16[8,32,128]{2,0,1:T(8,128)(2,1)} %get-tuple-element.4), channel_id=1, source_target_pairs={{0,24},{8,0},{16,8},{24,16},{1,25},{9,1},{17,9},{25,17},{2,26},{10... | collective-permute-start | bytes 196616 | tf_op jit(solution)/shard_map/ppermute | solution.py:19
  171.7 53.6 %collective-permute-start.17 = (bf16[8,32,128]{2,0,1:T(8,128)(2,1)}, bf16[8,32,128]{2,0,1:T(8,128)(2,1)}, u32[]{:S(2)}, u32[]{:S(2)}) collective-permute-start(bf16[8,32,128]{2,0,1:T(8,128)(2,1)} %collective-permute-done.15), channel_id=1, source_target_pairs={{0,8},{8,16},{16,24},{24,0},{1,9},{9,17},{17,25},{25,1},{2,10},{10... | collective-permute-start | bytes 196616 | tf_op jit(solution)/shard_map/ppermute | solution.py:16
  238.5 21.2 %copy-start.1 = (bf16[64,256]{1,0:T(8,128)(2,1)S(1)}, bf16[64,256]{1,0:T(8,128)(2,1)}, u32[]{:S(2)}) copy-start(bf16[64,256]{1,0:T(8,128)(2,1)} %param.9) | copy-start | bytes 98308
  (21 other events, 122.0 us)
Sparse Core Ops, SparseCore 0:
  27.0 25.5 reduce-scatter.2
  136.1 23.9 reduce-scatter.4
  165.6 54.9 all-reduce.1
